TPU v7x, 32 devices: a whole 2x2x4 slice. The times are simulated.
32 devices in a mesh: seq: 4 (over y, x), exp: 8 (over z, core).
Axes of the slice: x: 2, y: 2, z: 4, core: 2. Of those that a mesh axis runs over, the one named last changes fastest.
Arguments:
- token_ids: int32 [4, 32], replicated, may hold values from 0 to 51199
- cache_lengths: int32 [32], replicated, may hold values from 1 to 1024, as said below
- empty_blocks: int32 [32, 64], replicated, may hold values 0 or 1
- expert_ids: int32 [4, 32, 6], replicated, may hold values from 0 to 63, all different within a row
- embed_table: bfloat16 [51200, 2048], P(('seq', 'exp')), may hold values from -3 to 3
- attn_gain: float32 [2048], replicated, may hold values from 0.5 to 1.5
- w_query: bfloat16 [2048, 2048], P(None, 'seq'), may hold values from -0.125 to 0.125
- w_key: bfloat16 [2048, 2048], P(None, 'seq'), may hold values from -0.125 to 0.125
- w_value: bfloat16 [2048, 2048], P(None, 'seq'), may hold values from -0.125 to 0.125
- w_out: bfloat16 [2048, 2048], P('seq'), may hold values from -0.125 to 0.125
- k_cache: bfloat16 [32, 1024, 2048], P('exp', 'seq'), may hold values from -200 to 200
- v_cache: bfloat16 [32, 1024, 2048], P('exp', 'seq'), may hold values from -6 to 6
- moe_gain: float32 [2048], replicated, may hold values from 0.5 to 1.5
- w_router: bfloat16 [2048, 64], replicated, may hold values from -0.125 to 0.125
- gate_pieces: bfloat16 [256, 2048, 352], P(('seq', 'exp')), may hold values from -0.125 to 0.125
- up_pieces: bfloat16 [256, 2048, 352], P(('seq', 'exp')), may hold values from -0.125 to 0.125
- down_pieces: bfloat16 [256, 352, 2048], P(('seq', 'exp')), may hold values from -0.15625 to 0.15625
- shared_gate: bfloat16 [2048, 2816], P(None, 'exp'), may hold values from -0.125 to 0.125
- shared_up: bfloat16 [2048, 2816], P(None, 'exp'), may hold values from -0.125 to 0.125
- shared_down: bfloat16 [2816, 2048], P('exp'), may hold values from -0.109375 to 0.109375
- final_gain: float32 [2048], replicated, may hold values from 0.5 to 1.5
- w_head: bfloat16 [2048, 51200], P(None, ('seq', 'exp')), may hold values from -0.125 to 0.125
Outputs:
- hidden_norms: float32 [4, 32], replicated
- greatest_logits: float32 [4, 32], replicated
Inputs may be any that keep to these rules, and one draw needn't show every extreme that they name: `cache_lengths`: one of the 32 requests has exactly 1024 cached positions in every draw.
All inputs are finite; a program needn't handle non-finite values.
Results may differ from a plain program's by a relative error of at most 0.0055.
Values may be sent and summed in bfloat16 or wider, within the bound.
No kernel may reach another device: no remote copies, remote signals or barrier semaphores. Data moves between devices by JAX's collectives and lax.ppermute only.
A program may use at most 128 MiB of HBM per device.

v0:
```python
import math
import jax
import jax.numpy as jnp
from jax import lax
from jax.sharding import PartitionSpec as P

HDIM = 128
PIECES = 4
BLK = 16
epsilon = 1e-06
negative = -1e30


def rms_scale(values, scales):
    return values * lax.rsqrt(jnp.mean(values * values, axis=-1, keepdims=True) + epsilon) * scales


def rotate(values, places):
    half_width = values.shape[-1] // 2
    frequency = 10000.0 ** (-2.0 * jnp.arange(half_width, dtype=jnp.float32) / values.shape[-1])
    angles = places.astype(jnp.float32)[..., None, None] * frequency
    cosine_table = jnp.cos(angles)
    sine_table = jnp.sin(angles)
    lower = values[..., :half_width]
    upper = values[..., half_width:]
    return jnp.concatenate(
        [lower * cosine_table - upper * sine_table, upper * cosine_table + lower * sine_table],
        axis=-1,
    )


def joined(earlier, later):
    top_score = jnp.maximum(earlier[0], later[0])
    left_factor = jnp.exp(earlier[0] - top_score)
    right_factor = jnp.exp(later[0] - top_score)
    return (
        top_score,
        earlier[1] * left_factor + later[1] * right_factor,
        earlier[2] * left_factor[..., None] + later[2] * right_factor[..., None],
    )


def on_device(
    token_ids,
    cache_lengths,
    empty_blocks,
    expert_ids,
    embed_table,
    attn_gain,
    w_query,
    w_key,
    w_value,
    w_out,
    k_cache,
    v_cache,
    moe_gain,
    w_router,
    gate_pieces,
    up_pieces,
    down_pieces,
    shared_gate,
    shared_up,
    shared_down,
    final_gain,
    w_head,
):
    steps, requests = token_ids.shape
    tokens = steps * requests
    width = embed_table.shape[1]
    vocab_local = embed_table.shape[0]
    owner_index = lax.axis_index(("seq", "exp"))
    seq_index = lax.axis_index("seq")
    own_count = requests // lax.axis_size("exp")
    own_start = lax.axis_index("exp") * own_count
    local_ids = token_ids.reshape(tokens) - owner_index * vocab_local
    onehot = (local_ids[:, None] == jnp.arange(vocab_local, dtype=jnp.int32)[None, :]).astype(
        jnp.bfloat16
    )
    looked = jnp.dot(onehot, embed_table, preferred_element_type=jnp.float32).reshape(
        steps, requests, width
    )
    block_part = lax.psum_scatter(
        looked.astype(jnp.bfloat16), "exp", scatter_dimension=1, tiled=True
    )
    own_rows = lax.psum(block_part, "seq").astype(jnp.float32).reshape(steps * own_count, width)
    attn_in = rms_scale(own_rows, attn_gain).astype(jnp.bfloat16)
    own_lengths = lax.dynamic_slice_in_dim(cache_lengths, own_start, own_count, 0)
    places = (own_lengths[None, :] + jnp.arange(steps, dtype=jnp.int32)[:, None]).reshape(
        steps * own_count
    )
    heads_here = w_query.shape[1] // HDIM

    def project(weight):
        return jnp.dot(attn_in, weight, preferred_element_type=jnp.float32).reshape(
            steps * own_count, heads_here, HDIM
        )

    query_part = rotate(project(w_query), places).astype(jnp.bfloat16)
    key_part = rotate(project(w_key), places).astype(jnp.bfloat16)
    value_part = project(w_value).astype(jnp.bfloat16)
    queries, new_keys, new_values = (
        lax.all_gather(query_part, "seq", axis=1, tiled=True),
        lax.all_gather(key_part, "seq", axis=1, tiled=True),
        lax.all_gather(value_part, "seq", axis=1, tiled=True),
    )
    head_count = queries.shape[1]
    queries = queries.reshape(steps, own_count, head_count, HDIM)
    new_keys = new_keys.reshape(steps, own_count, head_count, HDIM)
    new_values = new_values.reshape(steps, own_count, head_count, HDIM)
    span = k_cache.shape[1]
    first_place = seq_index * span
    places_here = first_place + jnp.arange(span, dtype=jnp.int32)
    own_empty = lax.dynamic_slice_in_dim(empty_blocks, own_start, own_count, 0)
    local_blocks = lax.dynamic_slice_in_dim(own_empty, first_place // BLK, span // BLK, 1)
    blocked = jnp.broadcast_to(local_blocks[:, :, None], (own_count, span // BLK, BLK)).reshape(
        own_count, span
    )
    live_mask = ((places_here[None, :] < own_lengths[:, None]) & (blocked == 0))[None, :, None, :]
    cache_keys = k_cache.reshape(own_count, span, head_count, HDIM)
    cache_values = v_cache.reshape(own_count, span, head_count, HDIM)
    score_scale = 1.0 / math.sqrt(HDIM)
    cached = (
        jnp.einsum("trhd,rphd->trhp", queries, cache_keys, preferred_element_type=jnp.float32)
        * score_scale
    )
    local_top = jnp.max(jnp.where(live_mask, cached, negative), axis=3)
    top_score = lax.pmax(local_top, "seq")
    local_weights = jnp.where(live_mask, jnp.exp(cached - top_score[..., None]), 0.0)
    local_mixture = jnp.einsum(
        "trhp,rphd->trhd",
        local_weights.astype(jnp.bfloat16),
        cache_values,
        preferred_element_type=jnp.float32,
    )
    totals, mixture = (
        lax.psum(jnp.sum(local_weights, axis=3).astype(jnp.bfloat16), "seq").astype(jnp.float32),
        lax.psum(local_mixture.astype(jnp.bfloat16), "seq").astype(jnp.float32),
    )
    fresh_scores = (
        jnp.einsum("trhd,urhd->trhu", queries, new_keys, preferred_element_type=jnp.float32)
        * score_scale
    )
    causal = (jnp.arange(steps)[None, :] <= jnp.arange(steps)[:, None])[:, None, None, :]
    fresh_top = jnp.max(jnp.where(causal, fresh_scores, negative), axis=3)
    fresh_weights = jnp.where(causal, jnp.exp(fresh_scores - fresh_top[..., None]), 0.0)
    fresh_mixture = jnp.einsum(
        "trhu,urhd->trhd",
        fresh_weights.astype(jnp.bfloat16),
        new_values,
        preferred_element_type=jnp.float32,
    )
    top_score, totals, mixture = joined(
        (top_score, totals, mixture), (fresh_top, jnp.sum(fresh_weights, axis=3), fresh_mixture)
    )
    heads_out = (mixture / totals[..., None]).astype(jnp.bfloat16)
    own_heads = lax.dynamic_slice_in_dim(heads_out, seq_index * heads_here, heads_here, 2).reshape(
        steps * own_count, heads_here * HDIM
    )
    attn_sum = lax.psum(
        jnp.dot(own_heads, w_out, preferred_element_type=jnp.float32).astype(jnp.bfloat16), "seq"
    ).astype(jnp.float32)
    resid_own = own_rows + attn_sum
    resid_all = (
        lax.all_gather(
            resid_own.reshape(steps, own_count, width).astype(jnp.bfloat16),
            "exp",
            axis=1,
            tiled=True,
        )
        .astype(jnp.float32)
        .reshape(tokens, width)
    )
    moe_in = rms_scale(resid_all, moe_gain).astype(jnp.bfloat16)
    router = jax.nn.sigmoid(jnp.dot(moe_in, w_router, preferred_element_type=jnp.float32))
    expert_count = w_router.shape[1]
    chosen_ids = expert_ids.reshape(tokens, expert_ids.shape[2])
    picked = chosen_ids[:, :, None] == jnp.arange(expert_count, dtype=jnp.int32)[None, None, :]
    chosen = jnp.sum(jnp.where(picked, router[:, None, :], 0.0), axis=2)
    gate_weights = chosen / jnp.sum(chosen, axis=1, keepdims=True)
    rows_here = gate_pieces.shape[0]
    row_expert = (owner_index * rows_here + jnp.arange(rows_here, dtype=jnp.int32)) // PIECES
    token_weight = jnp.sum(
        jnp.where(
            chosen_ids[None, :, :] == row_expert[:, None, None], gate_weights[None, :, :], 0.0
        ),
        axis=2,
    )
    gate_out = jnp.einsum("nd,jdf->jnf", moe_in, gate_pieces, preferred_element_type=jnp.float32)
    up_out = jnp.einsum("nd,jdf->jnf", moe_in, up_pieces, preferred_element_type=jnp.float32)
    expert_hidden = (jax.nn.silu(gate_out) * up_out).astype(jnp.bfloat16)
    expert_out = jnp.einsum(
        "jnf,jfd->jnd", expert_hidden, down_pieces, preferred_element_type=jnp.float32
    )
    routed = jnp.einsum("jn,jnd->nd", token_weight, expert_out)
    share_count = tokens // lax.axis_size("seq")
    share_start = seq_index * share_count
    share_rows = lax.dynamic_slice_in_dim(moe_in, share_start, share_count, 0)
    shared_hidden = (
        jax.nn.silu(jnp.dot(share_rows, shared_gate, preferred_element_type=jnp.float32))
        * jnp.dot(share_rows, shared_up, preferred_element_type=jnp.float32)
    ).astype(jnp.bfloat16)
    shared_out = jnp.dot(shared_hidden, shared_down, preferred_element_type=jnp.float32)
    term_rows = lax.dynamic_update_slice_in_dim(
        routed,
        lax.dynamic_slice_in_dim(routed, share_start, share_count, 0) + shared_out,
        share_start,
        0,
    )
    final_hidden = resid_all + lax.psum(term_rows, ("seq", "exp"))
    hidden_norms = jnp.sqrt(jnp.mean(final_hidden * final_hidden, axis=-1)).reshape(steps, requests)
    head_in = rms_scale(final_hidden, final_gain).astype(jnp.bfloat16)
    local_best = jnp.max(jnp.dot(head_in, w_head, preferred_element_type=jnp.float32), axis=-1)
    greatest_logits = lax.pmax(local_best, ("seq", "exp")).reshape(steps, requests)
    return (hidden_norms, greatest_logits)


def solution(mesh):
    in_specs = (
        P(),
        P(),
        P(),
        P(),
        P(("seq", "exp"), None),
        P(),
        P(None, "seq"),
        P(None, "seq"),
        P(None, "seq"),
        P("seq", None),
        P("exp", "seq", None),
        P("exp", "seq", None),
        P(),
        P(),
        P(("seq", "exp"), None, None),
        P(("seq", "exp"), None, None),
        P(("seq", "exp"), None, None),
        P(None, "exp"),
        P(None, "exp"),
        P("exp", None),
        P(),
        P(None, ("seq", "exp")),
    )
    out_specs = (P(), P())
    return jax.shard_map(
        on_device, mesh=mesh, in_specs=in_specs, out_specs=out_specs, check_vma=False
    )
```

profile of v0, /device:TPU:0, one launch (start us, length us, event | category | flops | bytes accessed | tf_op | source)
XLA Modules:
  0.0 482.6 jit_solution(16864006460640909355)
XLA Ops:
  7.2 0.8 broadcast_subtract_fusion
  8.1 4.9 %convolution_convert_fusion = bf16[128,2048]{1,0:T(8,128)(2,1)} fusion(bf16[1600,2048]{1,0:T(8,128)(2,1)} %param.26, s32[128]{0:T(128)S(1)} %sub.51), kind=kOutput, calls=%fused_computation.8 | convolution fusion | flops 839327744 | bytes 7078400 | tf_op jit(solution)/shard_map/dot_general | solution.py:79
  13.1 0.8 dynamic-slice_compare_fusion
  14.3 4.0 copy.184
  18.2 3.9 copy.185
  22.3 4.0 copy.188
  26.4 0.6 dynamic-slice
  27.7 44.3 %all-reduce.15.cloned.1.call-done = bf16[4,32,2048]{2,1,0:T(8,128)(2,1)} async-done(((bf16[4,32,2048]{2,1,0:T(8,128)(2,1)}), bf16[4,32,2048]{2,1,0:T(8,128)(2,1)}) %all-reduce.15.cloned.1.call-update) | async-done | bytes 524304
  72.0 1.6 constant_dynamic-slice_fusion.3
  73.7 42.0 %all-reduce.7.cloned.1.call-done = bf16[4,4,2048]{2,1,0:T(4,128)(2,1)} async-done(((bf16[4,4,2048]{2,1,0:T(4,128)(2,1)}), bf16[4,4,2048]{2,1,0:T(4,128)(2,1)}) %all-reduce.7.cloned.1.call-update) | async-done | bytes 65552 | tf_op jit(solution)/shard_map/psum | solution.py:85
  115.6 1.0 multiply_reduce_fusion.2
  116.6 0.9 multiply_convert_fusion.2
  117.6 2.4 fusion.78
  120.0 0.7 fusion.79
  120.8 8.2 %all_gather.12 = bf16[16,16,128]{2,0,1:T(8,128)(2,1)S(1)} all-gather(bf16[16,4,128]{2,0,1:T(8,128)(2,1)S(1)} %pad_maximum_fusion), channel_id=1, replica_groups=mesh['seq'=4,'exp'=8] {'seq'}, dimensions={1}, use_global_device_ids=true | all-gather | bytes 81920 | tf_op jit(solution)/shard_map/all_gather | solution.py:102
  129.1 7.3 %all_gather.13 = bf16[16,16,128]{2,0,1:T(8,128)(2,1)S(1)} all-gather(bf16[16,4,128]{2,0,1:T(8,128)(2,1)S(1)} %pad_maximum_fusion.1), channel_id=1, replica_groups=mesh['seq'=4,'exp'=8] {'seq'}, dimensions={1}, use_global_device_ids=true | all-gather | bytes 81920 | tf_op jit(solution)/shard_map/all_gather | solution.py:103
  136.4 0.2 fusion.48
  137.1 3.5 select_reduce_fusion
  140.6 15.4 %pmax.14 = f32[4,4,16]{0,2,1:T(8,128)S(1)} all-reduce(f32[4,4,16]{0,2,1:T(8,128)S(1)} %get-tuple-element.21), channel_id=1, replica_groups=mesh['seq'=4,'exp'=8] {'seq'}, use_global_device_ids=true, to_apply=%region_4.5 | all-reduce | flops 256 | bytes 2048 | tf_op jit(solution)/shard_map/pmax | solution.py:127
  156.0 0.3 fusion.37
  156.2 3.5 fusion.21
  159.8 14.9 %psum.37 = bf16[4,4,16]{0,2,1:T(8,128)(2,1)S(1)} all-reduce(bf16[4,4,16]{0,2,1:T(8,128)(2,1)S(1)} %fusion.37), channel_id=1, replica_groups=mesh['seq'=4,'exp'=8] {'seq'}, use_global_device_ids=true, to_apply=%region_8.9 | all-reduce | flops 256 | bytes 1024 | tf_op jit(solution)/shard_map/psum | solution.py:136
  174.9 0.2 copy.174
  175.1 2.3 convolution_convert_fusion.2
  177.3 7.4 %all_gather.14 = bf16[16,16,128]{2,0,1:T(8,128)(2,1)S(1)} all-gather(bf16[16,4,128]{2,0,1:T(8,128)(2,1)S(1)} %convolution_convert_fusion.2), channel_id=1, replica_groups=mesh['seq'=4,'exp'=8] {'seq'}, dimensions={1}, use_global_device_ids=true | all-gather | bytes 81920 | tf_op jit(solution)/shard_map/all_gather | solution.py:104
  184.8 0.2 convolution_bitcast_fusion.2
  185.1 16.3 %all-reduce.9.cloned.1.call-done = bf16[4,4,16,128]{3,0,2,1:T(4,128)(2,1)} async-done(((bf16[4,4,16,128]{3,0,2,1:T(4,128)(2,1)}), bf16[4,4,16,128]{3,0,2,1:T(4,128)(2,1)}) %all-reduce.9.cloned.1.call-update) | async-done | bytes 65552 | tf_op jit(solution)/shard_map/psum | solution.py:137
  201.4 0.8 fusion.64
  202.2 1.0 convolution_convert_fusion.1
  203.4 42.5 %all-reduce.11.cloned.1.call-done = bf16[16,2048]{1,0:T(8,128)(2,1)} async-done(((bf16[16,2048]{1,0:T(8,128)(2,1)}), bf16[16,2048]{1,0:T(8,128)(2,1)}) %all-reduce.11.cloned.1.call-update) | async-done | bytes 65552 | tf_op jit(solution)/shard_map/psum | solution.py:159
  245.9 0.9 add_convert_fusion
  246.8 14.7 %all_gather.15 = bf16[4,32,2048]{2,0,1:T(4,128)(2,1)S(1)} all-gather(bf16[4,4,2048]{2,0,1:T(4,128)(2,1)S(1)} %copy.178), channel_id=1, replica_groups=mesh['seq'=4,'exp'=8] {'exp'}, dimensions={1}, use_global_device_ids=true | all-gather | bytes 589824 | tf_op jit(solution)/shard_map/all_gather | solution.py:164
  261.5 0.3 copy.179
  261.9 0.4 multiply_reduce_fusion.1
  262.6 6.3 %convolution_bitcast_fusion.1 = f32[8,128,352]{1,2,0:T(8,128)S(1)} fusion(bf16[8,2048,352]{1,2,0:T(8,128)(2,1)} %param.36, bf16[128,2048]{1,0:T(8,128)(2,1)S(1)} %fusion.29), kind=kOutput, calls=%fused_computation.13 | convolution fusion | flops 1476395008 | bytes 13500416 | tf_op jit(solution)/shard_map/nd,jdf->jnf/dot_general | solution.py:188
  268.8 0.3 fusion.27
  269.5 18.6 %fusion.11 = bf16[8,128,2048]{2,1,0:T(8,128)(2,1)} fusion(bf16[8,352,2048]{2,1,0:T(8,128)(2,1)} %param.38, bf16[8,2048,352]{1,2,0:T(8,128)(2,1)} %param.37, f32[8,128,352]{1,2,0:T(8,128)S(1)} %convolution_bitcast_fusion.1, bf16[128,2048]{1,0:T(8,128)(2,1)S(1)} %fusion.29), kind=kOutput, calls=%fused_computation.16 | convolution fusion | flops 2954952704 | bytes 29229056 | tf_op jit(solution)/shard_map/jnf,jfd->jnd/dot_general | solution.py:191
  288.1 5.3 %fusion = f32[128,1,2048]{2,1,0:T(1,128)S(1)} fusion(bf16[8,128,1]{0,2,1:T(2,128)(2,1)S(1)} %copy.181, bf16[8,128,2048]{2,1,0:T(8,128)(2,1)} %fusion.11), kind=kOutput, calls=%fused_computation | convolution fusion | flops 4194304 | bytes 5244928 | tf_op jit(solution)/shard_map/jn,jnd->nd/dot_general | solution.py:194
  293.4 0.3 copy.232
  293.8 1.0 copy-done.4
  294.8 0.5 fusion.45
  295.3 3.1 fusion.8
  298.5 1.0 copy-done.3
  299.5 130.2 %all-reduce.13.cloned.1.call-done = f32[128,2048]{1,0:T(8,128)} async-done(((f32[128,2048]{1,0:T(8,128)}), f32[128,2048]{1,0:T(8,128)}) %all-reduce.13.cloned.1.call-update) | async-done | bytes 1048592 | tf_op jit(solution)/shard_map/psum | solution.py:209
  429.7 1.4 bitcast_add_fusion
  431.2 5.0 %convolution_reduce_fusion = f32[128]{0:T(128)S(1)} fusion(bf16[2048,1600]{0,1:T(8,128)(2,1)} %param.43, f32[128,2048]{1,0:T(8,128)S(1)} %get-tuple-element.7, f32[2048]{0:T(1024)S(1)} %copy-done.7, f32[128]{0:T(128)S(1)} %get-tuple-element.19), kind=kOutput, calls=%fused_computation.17 | convolution fusion | flops 839851904 | bytes 7611392 | tf_op jit(solution)/shard_map/dot_general | solution.py:212
  436.3 39.1 %pmax.15 = f32[4,32]{1,0:T(4,128)} all-reduce(f32[4,32]{1,0:T(4,128)S(1)} %reshape.303), channel_id=1, replica_groups=mesh['seq'=4,'exp'=8] {'seq','exp'}, use_global_device_ids=true, to_apply=%region_18.19 | all-reduce | flops 128 | bytes 1024 | tf_op jit(solution)/shard_map/pmax | solution.py:213
  475.4 0.7 sqrt.8
  (75 shorter events, 2.9 us)
Async XLA Ops:
  7.2 195.1 %copy-start = (bf16[512,2048]{1,0:T(8,128)(2,1)S(1)}, bf16[512,2048]{1,0:T(8,128)(2,1)}, u32[]{:S(2)}) copy-start(bf16[512,2048]{1,0:T(8,128)(2,1)} %param.31) | copy-start | bytes 6291460
  7.2 64.8 %all-reduce.15.cloned.1.call-start = ((), (), s32[]{:S(2)}) async-start(), calls=%async_computation.4 | async-start | bytes 1048576
  8.1 5.9 %copy-start.11 = (s32[32]{0:T(128)S(1)}, s32[32]{0:T(128)}, u32[]{:S(2)}) copy-start(s32[32]{0:T(128)} %param.23) | copy-start | bytes 388
  13.0 102.6 %all-reduce.7.cloned.1.call-start = ((), (), s32[]{:S(2)}) async-start(), calls=%async_computation | async-start | bytes 131072 | tf_op jit(solution)/shard_map/psum | solution.py:85
  22.3 4.0 copy-start.8
  22.3 4.1 copy-start.12
  22.3 94.3 %copy-start.10 = (f32[2048]{0:T(1024)S(1)}, f32[2048]{0:T(1024)}, u32[]{:S(2)}) copy-start(f32[2048]{0:T(1024)} %param.27) | copy-start | bytes 24580
  73.6 127.8 %all-reduce.9.cloned.1.call-start = ((), (), s32[]{:S(2)}) async-start(), calls=%async_computation.1 | async-start | bytes 131072 | tf_op jit(solution)/shard_map/psum | solution.py:137
  117.6 2.4 copy-start.2
  159.8 86.1 %all-reduce.11.cloned.1.call-start = ((), (), s32[]{:S(2)}) async-start(), calls=%async_computation.2 | async-start | bytes 131072 | tf_op jit(solution)/shard_map/psum | solution.py:159
  175.1 28.3 %copy-start.5 = (bf16[4,4,2048]{2,1,0:T(4,128)(2,1)S(1)}, bf16[4,4,2048]{2,1,0:T(4,128)(2,1)}, u32[]{:S(2)}) copy-start(bf16[4,4,2048]{2,1,0:T(4,128)(2,1)} %all-reduce.7.cloned.1.call-done) | copy-start | bytes 196612
  203.2 59.1 %copy-start.9 = (f32[2048]{0:T(1024)S(1)}, f32[2048]{0:T(1024)}, u32[]{:S(2)}) copy-start(f32[2048]{0:T(1024)} %param.34) | copy-start | bytes 24580
  203.3 226.5 %all-reduce.13.cloned.1.call-start = ((), (), s32[]{:S(2)}) async-start(), calls=%async_computation.3 | async-start | bytes 2097152 | tf_op jit(solution)/shard_map/psum | solution.py:209
  262.6 6.3 %copy-start.6 = (bf16[2048,64]{0,1:T(8,128)(2,1)S(1)}, bf16[2048,64]{0,1:T(8,128)(2,1)}, u32[]{:S(2)}) copy-start(bf16[2048,64]{0,1:T(8,128)(2,1)} %param.35) | copy-start | bytes 786436
  293.4 1.4 copy-start.4
  298.4 1.0 copy-start.3
  298.5 132.7 %copy-start.7 = (f32[2048]{0:T(1024)S(1)}, f32[2048]{0:T(1024)}, u32[]{:S(2)}) copy-start(f32[2048]{0:T(1024)} %param.42) | copy-start | bytes 24580
  431.2 44.9 %copy-start.1 = (bf16[512,2048]{1,0:T(8,128)(2,1)S(1)}, bf16[512,2048]{1,0:T(8,128)(2,1)}, u32[]{:S(2)}) copy-start(bf16[512,2048]{1,0:T(8,128)(2,1)} %param.31) | copy-start | bytes 6291460
Sparse Core Ops, SparseCore 0:
  13.1 58.8 all-reduce.14
  75.1 40.4 all-reduce.6
  159.9 41.4 all-reduce.8
  204.3 41.4 all-reduce.10
  299.6 130.0 all-reduce.12
where the time goes:
time: 484 us; the launch traced here: 483 us
  waiting for transfers between devices  275 us (57%)
  blocking collectives  107 us (22%)
  matrix products  57.7 us (12%)
  local copies, waits for them, and re-layouts  19.1 us (4%)
  between operations  14.8 us (3%)
  other arithmetic  8.37 us (2%)
    psum x1, waiting for transfers between devices, on_device(): final_hidden = resid_all + lax.psum(term_rows, ('seq', 'exp'))  130 us
    unnamed x6, waiting for transfers between devices  44.4 us
    psum x1, waiting for transfers between devices, on_device(): lax.psum(jnp.dot(own_heads, w_out, preferred_element_type=jnp.float32).as...  42.5 us
    psum x1, waiting for transfers between devices, on_device(): lax.psum(block_part, 'seq').astype(jnp.float32)  42 us
    pmax x1, blocking collectives, on_device(): lax.pmax(local_best, ('seq', 'exp')).reshape(steps, requests)  39.1 us
    dot_general x1, matrix products, on_device(): jnp.einsum('jnf,jfd->jnd', expert_hidden, down_pieces, preferred_element_...  18.6 us
    psum x1, waiting for transfers between devices, on_device(): lax.psum(local_mixture.astype(jnp.bfloat16), 'seq').astype(jnp.float32)  16.3 us
    pmax x1, blocking collectives, on_device(): top_score = lax.pmax(local_top, 'seq')  15.4 us
  transfers between devices with their start and end apart: 5, of which 5 were waited for; matrix products, arithmetic and copies ran while one was open for 3% of the time, Pallas kernels for 0%

commit v1 on v0

--- a/solution.py
+++ b/solution.py
@@ -206,7 +206,7 @@
         share_start,
         0,
     )
-    final_hidden = resid_all + lax.psum(term_rows, ("seq", "exp"))
+    final_hidden = resid_all + lax.psum(lax.psum(term_rows, "exp"), "seq")
     hidden_norms = jnp.sqrt(jnp.mean(final_hidden * final_hidden, axis=-1)).reshape(steps, requests)
     head_in = rms_scale(final_hidden, final_gain).astype(jnp.bfloat16)
     local_best = jnp.max(jnp.dot(head_in, w_head, preferred_element_type=jnp.float32), axis=-1)

time: 484 us -> 467 us (0.965)
  waiting for transfers between devices: 275 us -> 259 us
    psum x1 -> x2, waiting for transfers between devices: 130 us -> 114 us  [on_device(): final_hidden = resid_all + lax.psum(lax.psum(term_rows, 'exp'), 'seq')]
    unnamed x6 -> x7, waiting for transfers between devices: 44.4 us -> 44.4 us
  transfers between devices with their start and end apart: 5 -> 6, of which waited for: 5 -> 6; matrix products, arithmetic and copies ran while one was open for 3% -> 4% of each run, Pallas kernels for 0% -> 0%
where the time goes in v1:
time: 467 us; the launch traced here: 466 us
  waiting for transfers between devices  259 us (55%)
  blocking collectives  107 us (23%)
  matrix products  57.7 us (12%)
  local copies, waits for them, and re-layouts  19.1 us (4%)
  between operations  15.1 us (3%)
  other arithmetic  8.37 us (2%)
    psum x2, waiting for transfers between devices, on_device(): final_hidden = resid_all + lax.psum(lax.psum(term_rows, 'exp'), 'seq')  114 us
    unnamed x7, waiting for transfers between devices  44.4 us
    psum x1, waiting for transfers between devices, on_device(): lax.psum(jnp.dot(own_heads, w_out, preferred_element_type=jnp.float32).as...  42.5 us
    psum x1, waiting for transfers between devices, on_device(): lax.psum(block_part, 'seq').astype(jnp.float32)  42 us
    pmax x1, blocking collectives, on_device(): lax.pmax(local_best, ('seq', 'exp')).reshape(steps, requests)  39.3 us
    dot_general x1, matrix products, on_device(): jnp.einsum('jnf,jfd->jnd', expert_hidden, down_pieces, preferred_element_...  18.6 us
    psum x1, waiting for transfers between devices, on_device(): lax.psum(local_mixture.astype(jnp.bfloat16), 'seq').astype(jnp.float32)  16.3 us
    pmax x1, blocking collectives, on_device(): top_score = lax.pmax(local_top, 'seq')  15.4 us
  transfers between devices with their start and end apart: 6, of which 6 were waited for; matrix products, arithmetic and copies ran while one was open for 4% of the time, Pallas kernels for 0%

profile of v1, /device:TPU:0, one launch (start us, length us, event | category | flops | bytes accessed | tf_op | source)
XLA Modules:
  0.0 466.4 jit_solution(5940974945236457855)
XLA Ops:
  7.2 0.8 broadcast_subtract_fusion
  8.1 4.9 %convolution_convert_fusion = bf16[128,2048]{1,0:T(8,128)(2,1)} fusion(bf16[1600,2048]{1,0:T(8,128)(2,1)} %param.26, s32[128]{0:T(128)S(1)} %sub.51), kind=kOutput, calls=%fused_computation.8 | convolution fusion | flops 839327744 | bytes 7078400 | tf_op jit(solution)/shard_map/dot_general | solution.py:79
  13.1 0.8 dynamic-slice_compare_fusion
  14.3 4.0 copy.184
  18.2 3.9 copy.185
  22.3 4.0 copy.188
  26.4 0.6 dynamic-slice
  27.7 44.3 %all-reduce.18.cloned.1.call-done = bf16[4,32,2048]{2,1,0:T(8,128)(2,1)} async-done(((bf16[4,32,2048]{2,1,0:T(8,128)(2,1)}), bf16[4,32,2048]{2,1,0:T(8,128)(2,1)}) %all-reduce.18.cloned.1.call-update) | async-done | bytes 524304
  72.0 1.6 constant_dynamic-slice_fusion.3
  73.7 42.0 %all-reduce.8.cloned.1.call-done = bf16[4,4,2048]{2,1,0:T(4,128)(2,1)} async-done(((bf16[4,4,2048]{2,1,0:T(4,128)(2,1)}), bf16[4,4,2048]{2,1,0:T(4,128)(2,1)}) %all-reduce.8.cloned.1.call-update) | async-done | bytes 65552 | tf_op jit(solution)/shard_map/psum | solution.py:85
  115.6 1.0 multiply_reduce_fusion.2
  116.6 0.9 multiply_convert_fusion.2
  117.6 2.4 fusion.78
  120.0 0.7 fusion.79
  120.8 8.2 %all_gather.12 = bf16[16,16,128]{2,0,1:T(8,128)(2,1)S(1)} all-gather(bf16[16,4,128]{2,0,1:T(8,128)(2,1)S(1)} %pad_maximum_fusion), channel_id=1, replica_groups=mesh['seq'=4,'exp'=8] {'seq'}, dimensions={1}, use_global_device_ids=true | all-gather | bytes 81920 | tf_op jit(solution)/shard_map/all_gather | solution.py:102
  129.1 7.3 %all_gather.13 = bf16[16,16,128]{2,0,1:T(8,128)(2,1)S(1)} all-gather(bf16[16,4,128]{2,0,1:T(8,128)(2,1)S(1)} %pad_maximum_fusion.1), channel_id=1, replica_groups=mesh['seq'=4,'exp'=8] {'seq'}, dimensions={1}, use_global_device_ids=true | all-gather | bytes 81920 | tf_op jit(solution)/shard_map/all_gather | solution.py:103
  136.4 0.2 fusion.48
  137.1 3.5 select_reduce_fusion
  140.6 15.4 %pmax.14 = f32[4,4,16]{0,2,1:T(8,128)S(1)} all-reduce(f32[4,4,16]{0,2,1:T(8,128)S(1)} %get-tuple-element.21), channel_id=1, replica_groups=mesh['seq'=4,'exp'=8] {'seq'}, use_global_device_ids=true, to_apply=%region_4.5 | all-reduce | flops 256 | bytes 2048 | tf_op jit(solution)/shard_map/pmax | solution.py:127
  156.0 0.3 fusion.37
  156.2 3.5 fusion.21
  159.8 14.9 %psum.44 = bf16[4,4,16]{0,2,1:T(8,128)(2,1)S(1)} all-reduce(bf16[4,4,16]{0,2,1:T(8,128)(2,1)S(1)} %fusion.37), channel_id=1, replica_groups=mesh['seq'=4,'exp'=8] {'seq'}, use_global_device_ids=true, to_apply=%region_8.9 | all-reduce | flops 256 | bytes 1024 | tf_op jit(solution)/shard_map/psum | solution.py:136
  175.1 2.3 convolution_convert_fusion.2
  177.3 7.4 %all_gather.14 = bf16[16,16,128]{2,0,1:T(8,128)(2,1)S(1)} all-gather(bf16[16,4,128]{2,0,1:T(8,128)(2,1)S(1)} %convolution_convert_fusion.2), channel_id=1, replica_groups=mesh['seq'=4,'exp'=8] {'seq'}, dimensions={1}, use_global_device_ids=true | all-gather | bytes 81920 | tf_op jit(solution)/shard_map/all_gather | solution.py:104
  184.8 0.2 convolution_bitcast_fusion.2
  185.1 16.3 %all-reduce.10.cloned.1.call-done = bf16[4,4,16,128]{3,0,2,1:T(4,128)(2,1)} async-done(((bf16[4,4,16,128]{3,0,2,1:T(4,128)(2,1)}), bf16[4,4,16,128]{3,0,2,1:T(4,128)(2,1)}) %all-reduce.10.cloned.1.call-update) | async-done | bytes 65552 | tf_op jit(solution)/shard_map/psum | solution.py:137
  201.4 0.8 fusion.64
  202.2 1.0 convolution_convert_fusion.1
  203.4 42.5 %all-reduce.12.cloned.1.call-done = bf16[16,2048]{1,0:T(8,128)(2,1)} async-done(((bf16[16,2048]{1,0:T(8,128)(2,1)}), bf16[16,2048]{1,0:T(8,128)(2,1)}) %all-reduce.12.cloned.1.call-update) | async-done | bytes 65552 | tf_op jit(solution)/shard_map/psum | solution.py:159
  245.9 0.9 add_convert_fusion
  246.8 14.7 %all_gather.15 = bf16[4,32,2048]{2,0,1:T(4,128)(2,1)S(1)} all-gather(bf16[4,4,2048]{2,0,1:T(4,128)(2,1)S(1)} %copy.178), channel_id=1, replica_groups=mesh['seq'=4,'exp'=8] {'exp'}, dimensions={1}, use_global_device_ids=true | all-gather | bytes 589824 | tf_op jit(solution)/shard_map/all_gather | solution.py:164
  261.5 0.3 copy.179
  261.9 0.4 multiply_reduce_fusion.1
  262.6 6.3 %convolution_bitcast_fusion.1 = f32[8,128,352]{1,2,0:T(8,128)S(1)} fusion(bf16[8,2048,352]{1,2,0:T(8,128)(2,1)} %param.36, bf16[128,2048]{1,0:T(8,128)(2,1)S(1)} %fusion.29), kind=kOutput, calls=%fused_computation.13 | convolution fusion | flops 1476395008 | bytes 13500416 | tf_op jit(solution)/shard_map/nd,jdf->jnf/dot_general | solution.py:188
  268.8 0.3 fusion.27
  269.5 18.6 %fusion.11 = bf16[8,128,2048]{2,1,0:T(8,128)(2,1)} fusion(bf16[8,352,2048]{2,1,0:T(8,128)(2,1)} %param.38, bf16[8,2048,352]{1,2,0:T(8,128)(2,1)} %param.37, f32[8,128,352]{1,2,0:T(8,128)S(1)} %convolution_bitcast_fusion.1, bf16[128,2048]{1,0:T(8,128)(2,1)S(1)} %fusion.29), kind=kOutput, calls=%fused_computation.16 | convolution fusion | flops 2954952704 | bytes 29229056 | tf_op jit(solution)/shard_map/jnf,jfd->jnd/dot_general | solution.py:191
  288.1 5.3 %fusion = f32[128,1,2048]{2,1,0:T(1,128)S(1)} fusion(bf16[8,128,1]{0,2,1:T(2,128)(2,1)S(1)} %copy.181, bf16[8,128,2048]{2,1,0:T(8,128)(2,1)} %fusion.11), kind=kOutput, calls=%fused_computation | convolution fusion | flops 4194304 | bytes 5244928 | tf_op jit(solution)/shard_map/jn,jnd->nd/dot_general | solution.py:194
  293.4 0.3 copy.232
  293.8 1.0 copy-done.4
  294.8 0.5 fusion.45
  295.3 3.1 fusion.8
  298.5 1.0 copy-done.3
  299.6 59.1 %all-reduce.14.cloned.1.call-done = f32[128,2048]{1,0:T(8,128)} async-done(((f32[128,2048]{1,0:T(8,128)}), f32[128,2048]{1,0:T(8,128)}) %all-reduce.14.cloned.1.call-update) | async-done | bytes 1048592 | tf_op jit(solution)/shard_map/psum | solution.py:209
  358.7 54.4 %all-reduce.16.cloned.1.call-done = f32[128,2048]{1,0:T(8,128)} async-done(((f32[128,2048]{1,0:T(8,128)}), f32[128,2048]{1,0:T(8,128)}) %all-reduce.16.cloned.1.call-update) | async-done | bytes 1048592 | tf_op jit(solution)/shard_map/psum | solution.py:209
  413.1 1.4 bitcast_add_fusion
  414.6 5.0 %convolution_reduce_fusion = f32[128]{0:T(128)S(1)} fusion(bf16[2048,1600]{0,1:T(8,128)(2,1)} %param.43, f32[128,2048]{1,0:T(8,128)S(1)} %get-tuple-element.7, f32[2048]{0:T(1024)S(1)} %copy-done.7, f32[128]{0:T(128)S(1)} %get-tuple-element.19), kind=kOutput, calls=%fused_computation.17 | convolution fusion | flops 839851904 | bytes 7611392 | tf_op jit(solution)/shard_map/dot_general | solution.py:212
  419.7 39.3 %pmax.15 = f32[4,32]{1,0:T(4,128)} all-reduce(f32[4,32]{1,0:T(4,128)S(1)} %reshape.303), channel_id=1, replica_groups=mesh['seq'=4,'exp'=8] {'seq','exp'}, use_global_device_ids=true, to_apply=%region_19.20 | all-reduce | flops 128 | bytes 1024 | tf_op jit(solution)/shard_map/pmax | solution.py:213
  458.9 0.7 sqrt.8
  (78 shorter events, 3.2 us)
Async XLA Ops:
  7.2 195.1 %copy-start = (bf16[512,2048]{1,0:T(8,128)(2,1)S(1)}, bf16[512,2048]{1,0:T(8,128)(2,1)}, u32[]{:S(2)}) copy-start(bf16[512,2048]{1,0:T(8,128)(2,1)} %param.31) | copy-start | bytes 6291460
  7.2 64.8 %all-reduce.18.cloned.1.call-start = ((), (), s32[]{:S(2)}) async-start(), calls=%async_computation.5 | async-start | bytes 1048576
  8.1 5.9 %copy-start.11 = (s32[32]{0:T(128)S(1)}, s32[32]{0:T(128)}, u32[]{:S(2)}) copy-start(s32[32]{0:T(128)} %param.23) | copy-start | bytes 388
  13.0 102.6 %all-reduce.8.cloned.1.call-start = ((), (), s32[]{:S(2)}) async-start(), calls=%async_computation | async-start | bytes 131072 | tf_op jit(solution)/shard_map/psum | solution.py:85
  22.3 4.0 copy-start.8
  22.3 4.1 copy-start.12
  22.3 94.3 %copy-start.10 = (f32[2048]{0:T(1024)S(1)}, f32[2048]{0:T(1024)}, u32[]{:S(2)}) copy-start(f32[2048]{0:T(1024)} %param.27) | copy-start | bytes 24580
  73.6 127.8 %all-reduce.10.cloned.1.call-start = ((), (), s32[]{:S(2)}) async-start(), calls=%async_computation.1 | async-start | bytes 131072 | tf_op jit(solution)/shard_map/psum | solution.py:137
  117.6 2.4 copy-start.2
  159.8 86.1 %all-reduce.12.cloned.1.call-start = ((), (), s32[]{:S(2)}) async-start(), calls=%async_computation.2 | async-start | bytes 131072 | tf_op jit(solution)/shard_map/psum | solution.py:159
  175.1 28.3 %copy-start.5 = (bf16[4,4,2048]{2,1,0:T(4,128)(2,1)S(1)}, bf16[4,4,2048]{2,1,0:T(4,128)(2,1)}, u32[]{:S(2)}) copy-start(bf16[4,4,2048]{2,1,0:T(4,128)(2,1)} %all-reduce.8.cloned.1.call-done) | copy-start | bytes 196612
  203.2 59.1 %copy-start.9 = (f32[2048]{0:T(1024)S(1)}, f32[2048]{0:T(1024)}, u32[]{:S(2)}) copy-start(f32[2048]{0:T(1024)} %param.34) | copy-start | bytes 24580
  203.3 155.4 %all-reduce.14.cloned.1.call-start = ((), (), s32[]{:S(2)}) async-start(), calls=%async_computation.3 | async-start | bytes 2097152 | tf_op jit(solution)/shard_map/psum | solution.py:209
  262.6 6.3 %copy-start.6 = (bf16[2048,64]{0,1:T(8,128)(2,1)S(1)}, bf16[2048,64]{0,1:T(8,128)(2,1)}, u32[]{:S(2)}) copy-start(bf16[2048,64]{0,1:T(8,128)(2,1)} %param.35) | copy-start | bytes 786436
  293.4 1.4 copy-start.4
  298.4 1.0 copy-start.3
  299.5 113.6 %all-reduce.16.cloned.1.call-start = ((), (), s32[]{:S(2)}) async-start(), calls=%async_computation.4 | async-start | bytes 2097152 | tf_op jit(solution)/shard_map/psum | solution.py:209
  358.7 55.9 %copy-start.7 = (f32[2048]{0:T(1024)S(1)}, f32[2048]{0:T(1024)}, u32[]{:S(2)}) copy-start(f32[2048]{0:T(1024)} %param.42) | copy-start | bytes 24580
  414.6 45.0 %copy-start.1 = (bf16[512,2048]{1,0:T(8,128)(2,1)S(1)}, bf16[512,2048]{1,0:T(8,128)(2,1)}, u32[]{:S(2)}) copy-start(bf16[512,2048]{1,0:T(8,128)(2,1)} %param.31) | copy-start | bytes 6291460
Sparse Core Ops, SparseCore 0:
  13.1 58.8 all-reduce.17
  75.1 40.4 all-reduce.7
  159.9 41.4 all-reduce.9
  204.3 41.4 all-reduce.11
  299.6 58.9 all-reduce.13
  361.6 51.4 all-reduce.15
